TPU v7x, 32 devices: a whole 2x2x4 slice. The times are simulated.
32 devices in a mesh: expert: 4 (over z), shard: 8 (over y, x, core).
Axes of the slice: x: 2, y: 2, z: 4, core: 2. Of those that a mesh axis runs over, the one named last changes fastest.
Arguments:
- tokens: bfloat16 [18912, 768], P(('expert', 'shard')), may hold values from -6 to 6
- image_counts: int32 [4, 8], P('expert', 'shard'), may hold values from 1 to 3, as said below
- routes: int32 [18912, 2], P(('expert', 'shard')), may hold values from 0 to 3, all different within a row; in each aligned block of 591 rows (0 to 590, 591 to 1181, ...) at most 376 rows name the same one
- w_qkv: bfloat16 [768, 2304], P('shard'), may hold values from -0.21875 to 0.21875
- w_out: bfloat16 [768, 768], P('shard'), may hold values from -1.5 to 1.5
- w_router: bfloat16 [768, 4], P('shard'), may hold values from -0.15625 to 0.15625
- gain_attn: bfloat16 [768], P('shard'), may hold values from 0.25 to 1.75
- gain_moe: bfloat16 [768], P('shard'), may hold values from 0.25 to 1.75
- w_in: bfloat16 [4, 768, 3072], P('expert', 'shard'), may hold values from -0.21875 to 0.21875
- w_back: bfloat16 [4, 3072, 768], P('expert', 'shard'), may hold values from -0.625 to 0.625
- cotangent: bfloat16 [18912, 768], P(('expert', 'shard')), may hold values from -6 to 6
Outputs:
- output: bfloat16 [18912, 768], P(('expert', 'shard'))
- grad_tokens: bfloat16 [18912, 768], P(('expert', 'shard'))
- grad_w_qkv: float32 [768, 2304], P('shard')
- grad_w_out: float32 [768, 768], P('shard')
- grad_w_router: float32 [768, 4], P('shard')
- grad_gain_attn: float32 [768], P('shard')
- grad_gain_moe: float32 [768], P('shard')
- grad_w_in: float32 [4, 768, 3072], P('expert', 'shard')
- grad_w_back: float32 [4, 3072, 768], P('expert', 'shard')
Inputs may be any that keep to these rules, and one draw needn't show every extreme that they name: `image_counts`: each device holds between 1 and 3 live images; some device holds 3 and some holds 1. `routes`: the two experts of a token differ; among the rows of one device at most 376 name any one expert.
All inputs are finite; a program needn't handle non-finite values.
Results may differ from a plain program's by a relative error of at most 0.024.
Values may be sent and summed in bfloat16 or wider, within the bound.
No kernel may reach another device: no remote copies, remote signals or barrier semaphores. Data moves between devices by JAX's collectives and lax.ppermute only.
A program may use at most 256 MiB of HBM per device.

v0:
```python
import jax
import jax.numpy as jnp
from jax import lax
from jax.sharding import PartitionSpec as P

H = 12
HD = 64
SEQ = 197
EPSILON = 1e-06
ROW_CONTRACT = (((0,), (0,)), ((), ()))
COL_CONTRACT = (((1,), (1,)), ((), ()))


def layer_norm(values, norm_gain):
    row_mean = jnp.mean(values, axis=-1, keepdims=True)
    centered = values - row_mean
    variance = jnp.mean(centered * centered, axis=-1, keepdims=True)
    return centered * lax.rsqrt(variance + EPSILON) * norm_gain


def normalize_rows(scores):
    row_top = jnp.max(scores, axis=-1, keepdims=True)
    exp_scores = jnp.exp(scores - row_top)
    return exp_scores / jnp.sum(exp_scores, axis=-1, keepdims=True)


def gelu_exact(values):
    return jax.nn.gelu(values, approximate=False)


def shards(
    tokens,
    image_counts,
    routes,
    w_qkv,
    w_out,
    w_router,
    gain_attn,
    gain_moe,
    w_in,
    w_back,
    cotangent,
):
    rows, width = tokens.shape
    experts = lax.axis_size("expert")
    capacity = 8 * (5 * rows // (16 * experts)) + 8
    overflow = experts * capacity
    images = rows // SEQ
    score_scale = HD ** (-0.5)
    row_ids = jnp.arange(rows, dtype=jnp.int32)
    live_int = (row_ids // SEQ < image_counts[0, 0]).astype(jnp.int32)
    live_rows = live_int.astype(jnp.float32)
    full_qkv, full_out, full_router, full_gain_attn, full_gain_moe = (
        lax.all_gather(w_qkv, "shard", axis=0, tiled=True),
        lax.all_gather(w_out, "shard", axis=0, tiled=True),
        lax.all_gather(w_router, "shard", axis=0, tiled=True),
        lax.all_gather(gain_attn, "shard", axis=0, tiled=True),
        lax.all_gather(gain_moe, "shard", axis=0, tiled=True),
    )
    gain_one = full_gain_attn.astype(jnp.float32)
    gain_two = full_gain_moe.astype(jnp.float32)
    gathered = (
        lax.all_gather(w_in, "shard", axis=1, tiled=True),
        lax.all_gather(w_back, "shard", axis=1, tiled=True),
    )
    expert_first = gathered[0][0]
    expert_second = gathered[1][0]
    token_f = tokens.astype(jnp.float32)
    attn_in = layer_norm(token_f, gain_one).astype(jnp.bfloat16)
    projected = jnp.dot(attn_in, full_qkv, preferred_element_type=jnp.float32).astype(jnp.bfloat16)
    split_heads = projected.reshape(images, SEQ, 3, H, HD)
    queries = split_heads[:, :, 0]
    keys_part = split_heads[:, :, 1]
    values_part = split_heads[:, :, 2]
    scores = (
        jnp.einsum("ishd,ithd->ihst", queries, keys_part, preferred_element_type=jnp.float32)
        * score_scale
    )
    row_top = jnp.max(scores, axis=-1, keepdims=True)
    log_total = row_top + jnp.log(jnp.sum(jnp.exp(scores - row_top), axis=-1, keepdims=True))
    attn_probs = jnp.exp(scores - log_total)
    mixed_rows = (
        jnp.einsum(
            "ihst,ithd->ishd",
            attn_probs.astype(jnp.bfloat16),
            values_part,
            preferred_element_type=jnp.float32,
        )
        .reshape(rows, width)
        .astype(jnp.bfloat16)
    )
    hidden_state = token_f + jnp.dot(mixed_rows, full_out, preferred_element_type=jnp.float32)
    moe_in = layer_norm(hidden_state, gain_two).astype(jnp.bfloat16)
    logits = jnp.dot(moe_in, full_router, preferred_element_type=jnp.float32)
    router_probs = normalize_rows(logits)
    expert_ids = jnp.arange(experts, dtype=jnp.int32)
    choose = (routes[:, :, None] == expert_ids).astype(jnp.float32)
    chosen = jnp.sum(choose * router_probs[:, None, :], axis=2)
    pick_table = (routes[:, :, None] == expert_ids).astype(jnp.int32) * live_int[:, None, None]
    flat_picks = pick_table.reshape(rows * 2, experts)
    before = jnp.cumsum(flat_picks, axis=0) - flat_picks
    slot_index = jnp.sum(before * flat_picks, axis=1).reshape(rows, 2)
    position = jnp.where(live_int[:, None] > 0, routes * capacity + slot_index, overflow)
    safe_index = jnp.minimum(position, overflow - 1)
    outgoing = jnp.zeros((overflow, width), jnp.bfloat16)
    outgoing = (
        outgoing.at[position[:, 0]]
        .set(moe_in, mode="drop")
        .at[position[:, 1]]
        .set(moe_in, mode="drop")
    )
    outgoing = outgoing.reshape(experts, capacity, width)
    arrived = lax.all_to_all(outgoing, "expert", split_axis=0, concat_axis=0, tiled=True)
    sources = arrived.shape[0]
    slot_count = arrived.shape[1]
    flat_rows = arrived.reshape(sources * slot_count, width)
    pre_act = jnp.dot(flat_rows, expert_first, preferred_element_type=jnp.float32)
    activated = gelu_exact(pre_act).astype(jnp.bfloat16)
    produced = jnp.dot(activated, expert_second, preferred_element_type=jnp.float32).astype(
        jnp.bfloat16
    )
    produced, pre_act, activated, arrived = (
        produced.reshape(sources, slot_count, width),
        pre_act.reshape(sources, slot_count, -1),
        activated.reshape(sources, slot_count, -1),
        arrived,
    )
    returned = lax.all_to_all(produced, "expert", split_axis=0, concat_axis=0, tiled=True)
    picked = returned.reshape(overflow, width)[safe_index].astype(jnp.float32)
    weighted = chosen * live_rows[:, None]
    moe_out = jnp.sum(weighted[:, :, None] * picked, axis=1)
    output = (live_rows[:, None] * (hidden_state + moe_out)).astype(jnp.bfloat16)
    grad_out = cotangent.astype(jnp.float32) * live_rows[:, None]
    grad_chosen = jnp.sum(grad_out[:, None, :] * picked, axis=2) * live_rows[:, None]
    grad_picked = (weighted[:, :, None] * grad_out[:, None, :]).astype(jnp.bfloat16)
    back_out = jnp.zeros((overflow, width), jnp.bfloat16)
    back_out = (
        back_out.at[position[:, 0]]
        .set(grad_picked[:, 0], mode="drop")
        .at[position[:, 1]]
        .set(grad_picked[:, 1], mode="drop")
    )
    arriving_grad = lax.all_to_all(
        back_out.reshape(experts, capacity, width),
        "expert",
        split_axis=0,
        concat_axis=0,
        tiled=True,
    )
    regathered = (
        lax.all_gather(w_in, "shard", axis=1, tiled=True),
        lax.all_gather(w_back, "shard", axis=1, tiled=True),
    )
    back_first = regathered[0][0]
    back_second = regathered[1][0]
    flat_grad = arriving_grad.reshape(overflow, width)
    flat_pre = pre_act.reshape(overflow, -1)
    flat_act = activated.reshape(overflow, -1)
    flat_arrived = arrived.reshape(overflow, width)
    grad_second = lax.dot_general(
        flat_act, flat_grad, ROW_CONTRACT, preferred_element_type=jnp.float32
    )
    hidden_grad = lax.dot_general(
        flat_grad, back_second, COL_CONTRACT, preferred_element_type=jnp.float32
    )
    gelu_value, gelu_back = jax.vjp(gelu_exact, flat_pre)
    pre_grad = gelu_back(hidden_grad)[0].astype(jnp.bfloat16)
    grad_first = lax.dot_general(
        flat_arrived, pre_grad, ROW_CONTRACT, preferred_element_type=jnp.float32
    )
    row_grad = lax.dot_general(
        pre_grad, back_first, COL_CONTRACT, preferred_element_type=jnp.float32
    ).astype(jnp.bfloat16)
    back_rows = lax.all_to_all(
        row_grad.reshape(experts, capacity, width),
        "expert",
        split_axis=0,
        concat_axis=0,
        tiled=True,
    )
    incoming = back_rows.reshape(overflow, width)[safe_index].astype(jnp.float32)
    expert_part = jnp.sum(incoming, axis=1) * live_rows[:, None]
    prob_sum = jnp.sum(choose * grad_chosen[:, :, None], axis=1)
    logit_grad = (
        router_probs * (prob_sum - jnp.sum(router_probs * prob_sum, axis=-1, keepdims=True))
    ).astype(jnp.bfloat16)
    grad_router = lax.dot_general(
        moe_in, logit_grad, ROW_CONTRACT, preferred_element_type=jnp.float32
    )
    moe_in_grad = expert_part + lax.dot_general(
        logit_grad, full_router, COL_CONTRACT, preferred_element_type=jnp.float32
    )
    norm_value, norm_back = jax.vjp(layer_norm, hidden_state, gain_two)
    state_part, grad_gain_two = norm_back(moe_in_grad)
    state_grad = grad_out + state_part
    branch_grad = state_grad.astype(jnp.bfloat16)
    grad_wout = lax.dot_general(
        mixed_rows, branch_grad, ROW_CONTRACT, preferred_element_type=jnp.float32
    )
    mixed_grad = lax.dot_general(
        branch_grad, full_out, COL_CONTRACT, preferred_element_type=jnp.float32
    )
    mixed_grad = mixed_grad.astype(jnp.bfloat16).reshape(images, SEQ, H, HD)
    again_scores = (
        jnp.einsum("ishd,ithd->ihst", queries, keys_part, preferred_element_type=jnp.float32)
        * score_scale
    )
    again_probs = jnp.exp(again_scores - log_total)
    grad_values = jnp.einsum(
        "ihst,ishd->ithd",
        again_probs.astype(jnp.bfloat16),
        mixed_grad,
        preferred_element_type=jnp.float32,
    )
    prob_grad = jnp.einsum(
        "ishd,ithd->ihst", mixed_grad, values_part, preferred_element_type=jnp.float32
    )
    score_grad = (
        again_probs * (prob_grad - jnp.sum(again_probs * prob_grad, axis=-1, keepdims=True))
    ).astype(jnp.bfloat16)
    grad_queries = (
        jnp.einsum("ihst,ithd->ishd", score_grad, keys_part, preferred_element_type=jnp.float32)
        * score_scale
    )
    grad_keys = (
        jnp.einsum("ihst,ishd->ithd", score_grad, queries, preferred_element_type=jnp.float32)
        * score_scale
    )
    projected_grad = (
        jnp.stack([grad_queries, grad_keys, grad_values], axis=2)
        .reshape(rows, 3 * width)
        .astype(jnp.bfloat16)
    )
    grad_qkv = lax.dot_general(
        attn_in, projected_grad, ROW_CONTRACT, preferred_element_type=jnp.float32
    )
    attn_in_grad = lax.dot_general(
        projected_grad, full_qkv, COL_CONTRACT, preferred_element_type=jnp.float32
    )
    first_value, first_back = jax.vjp(layer_norm, token_f, gain_one)
    token_part, grad_gain_one = first_back(attn_in_grad)
    grad_tokens = (state_grad + token_part).astype(jnp.bfloat16)
    grad_in_share, grad_back_share = (
        lax.psum_scatter(
            grad_first[None].astype(jnp.bfloat16), "shard", scatter_dimension=1, tiled=True
        ).astype(jnp.float32),
        lax.psum_scatter(
            grad_second[None].astype(jnp.bfloat16), "shard", scatter_dimension=1, tiled=True
        ).astype(jnp.float32),
    )
    shares = (
        lax.psum_scatter(
            grad_qkv.astype(jnp.bfloat16), "shard", scatter_dimension=0, tiled=True
        ).astype(jnp.float32),
        lax.psum_scatter(
            grad_wout.astype(jnp.bfloat16), "shard", scatter_dimension=0, tiled=True
        ).astype(jnp.float32),
        lax.psum_scatter(
            grad_router.astype(jnp.bfloat16), "shard", scatter_dimension=0, tiled=True
        ).astype(jnp.float32),
        lax.psum_scatter(
            grad_gain_one.astype(jnp.bfloat16), "shard", scatter_dimension=0, tiled=True
        ).astype(jnp.float32),
        lax.psum_scatter(
            grad_gain_two.astype(jnp.bfloat16), "shard", scatter_dimension=0, tiled=True
        ).astype(jnp.float32),
    )
    totals = (
        lax.psum(shares[0].astype(jnp.bfloat16), "expert").astype(jnp.float32),
        lax.psum(shares[1].astype(jnp.bfloat16), "expert").astype(jnp.float32),
        lax.psum(shares[2].astype(jnp.bfloat16), "expert").astype(jnp.float32),
        lax.psum(shares[3].astype(jnp.bfloat16), "expert").astype(jnp.float32),
        lax.psum(shares[4].astype(jnp.bfloat16), "expert").astype(jnp.float32),
    )
    return (
        output,
        grad_tokens,
        totals[0],
        totals[1],
        totals[2],
        totals[3],
        totals[4],
        grad_in_share,
        grad_back_share,
    )


def solution(mesh):
    return jax.shard_map(
        shards,
        mesh=mesh,
        in_specs=(
            P(("expert", "shard"), None),
            P("expert", "shard"),
            P(("expert", "shard"), None),
            P("shard", None),
            P("shard", None),
            P("shard", None),
            P("shard"),
            P("shard"),
            P("expert", "shard", None),
            P("expert", "shard", None),
            P(("expert", "shard"), None),
        ),
        out_specs=(
            P(("expert", "shard"), None),
            P(("expert", "shard"), None),
            P("shard", None),
            P("shard", None),
            P("shard", None),
            P("shard"),
            P("shard"),
            P("expert", "shard", None),
            P("expert", "shard", None),
        ),
        check_vma=False,
    )
```

profile of v0, /device:TPU:0, one launch (start us, length us, event | category | flops | bytes accessed | tf_op | source)
XLA Modules:
  0.0 760.9 jit_solution(17173408247433804776)
XLA Ops:
  9.4 1.3 fusion.75
  13.1 15.5 %all-reduce.6 = (bf16[768]{0:T(1024)(128)(2,1)S(1)}, bf16[768]{0:T(1024)(128)(2,1)S(1)}) all-reduce(bf16[768]{0:T(1024)(128)(2,1)S(1)} %dynamic-update-slice, bf16[768]{0:T(1024)(128)(2,1)S(1)} %dynamic-update-slice.1), channel_id=1, replica_groups=mesh['expert'=4,'shard'=8] {'shard'}, use_global_device_ids=true, to_apply=%add.1 | all-reduce | flops 1536 | bytes 6144
  34.2 12.4 %all-gather.6.cloned.1.call-done = bf16[768,2304]{1,0:T(8,128)(2,1)} async-done(((bf16[96,2304]{1,0:T(8,128)(2,1)}), bf16[768,2304]{1,0:T(8,128)(2,1)}) %all-gather.6.cloned.1.call-update) | async-done | bytes 3538960 | tf_op jit(solution)/shard_map/all_gather | solution.py:54
  46.6 6.0 convolution_convert_fusion.3
  52.6 9.3 %reshape.295 = bf16[3,197,3,12,64]{4,3,2,1,0:T(8,128)(2,1)} reshape(bf16[591,2304]{1,0:T(8,128)(2,1)} %convolution_convert_fusion.3) | data formatting | bytes 5446656 | tf_op jit(solution)/shard_map/reshape | solution.py:71
  61.8 6.7 fusion.74
  68.5 4.2 copy.146
  72.7 4.2 copy.147
  76.9 3.5 copy.145
  80.4 3.4 multiply_reduce_fusion.1
  83.9 1.6 exponential_reduce_fusion
  87.4 1.6 fusion.34
  90.0 2.1 convert_element_type.167
  92.1 2.6 fusion.76
  95.0 8.0 %scatter_custom_fusion = bf16[1504,768]{1,0:T(8,128)(2,1)} fusion(s32[591]{0:T(1024)S(1)} %get-tuple-element.16, bf16[]{:T(256)} %constant.53.clone.1, f32[591,768]{1,0:T(8,128)S(1)} %get-tuple-element.42, f32[768]{0:T(1024)S(1)} %convert_element_type.168, f32[591]{0:T(1024)S(1)} %fusion.63, f32[591]{0:T(1024)S(1)} %broadcast_multiply_fusion.2), kind=kCustom, calls=%fused_computation.92 | custom fusion | flops 1815552 | bytes 4141058 | tf_op jit(solution)/shard_map/scatter | solution.py:108
  103.1 9.9 %scatter_custom_fusion.1 = bf16[1504,768]{1,0:T(8,128)(2,1)} fusion(bf16[1504,768]{1,0:T(8,128)(2,1)} %scatter_custom_fusion, s32[591]{0:T(1024)S(1)} %get-tuple-element.15, f32[591,768]{1,0:T(8,128)S(1)} %get-tuple-element.42, f32[768]{0:T(1024)S(1)} %convert_element_type.168, f32[591]{0:T(1024)S(1)} %fusion.63, f32[591]{0:T(1024)S(1)} %broadcast_multiply_fusion.2), kind=kCustom, calls=%fused_computation.155 | custom fusion | flops 1815552 | bytes 4141056 | tf_op jit(solution)/shard_map/scatter | solution.py:110
  113.0 4.6 all-to-all-start
  118.2 52.6 %all-to-all-done = bf16[4,376,768]{2,1,0:T(8,128)(2,1)S(1)} async-done(((bf16[4,376,768]{2,1,0:T(8,128)(2,1)}), bf16[4,376,768]{2,1,0:T(8,128)(2,1)S(1)}, u32[]{:S(2)}, u32[]{:S(2)}) %all-to-all-start) | async-done | bytes 2310176 | tf_op jit(solution)/shard_map/all_to_all | solution.py:113
  170.8 47.9 %multiply_convert_fusion = (bf16[1504,3072]{1,0:T(8,128)(2,1)}, f32[1504,3072]{1,0:T(8,128)}, f32[1504,3072]{1,0:T(8,128)}) fusion(bf16[1504,768]{1,0:T(8,128)(2,1)S(1)} %bitcast.123, bf16[1,768,3072]{2,1,0:T(8,128)(2,1)} %all-gather.10.cloned.1.call-done), kind=kOutput, calls=%fused_computation.9 | convolution fusion | flops 7397081088 | bytes 53231616 | tf_op jit(solution)/shard_map/dot_general | solution.py:117
  218.7 12.3 %fusion.19 = bf16[1504,768]{1,0:T(8,128)(2,1)} fusion(bf16[1504,3072]{1,0:T(8,128)(2,1)} %get-tuple-element.30, bf16[1,3072,768]{2,1,0:T(8,128)(2,1)} %all-gather.12.cloned.1.call-done), kind=kOutput, calls=%fused_computation.47 | convolution fusion | flops 7097917440 | bytes 16269312 | tf_op jit(solution)/shard_map/dot_general | solution.py:119
  231.0 3.8 all-to-all-start.1
  234.8 9.4 %all-gather = bf16[8,96,4]{1,2,0:T(4,128)(2,1)S(1)} all-gather(bf16[1,96,4]{1,2,0:T(4,128)(2,1)S(1)} %bitcast.131), channel_id=1, replica_groups=mesh['expert'=4,'shard'=8] {'shard'}, dimensions={0}, use_global_device_ids=true | all-gather | bytes 6912 | tf_op jit(solution)/shard_map/all_gather | solution.py:56
  246.8 1.5 convert_multiply_fusion
  249.1 38.0 %all-to-all-done.1 = bf16[4,376,768]{2,1,0:T(8,128)(2,1)S(1)} async-done(((bf16[4,376,768]{2,1,0:T(8,128)(2,1)}), bf16[4,376,768]{2,1,0:T(8,128)(2,1)S(1)}, u32[]{:S(2)}, u32[]{:S(2)}) %all-to-all-start.1) | async-done | bytes 2310176 | tf_op jit(solution)/shard_map/all_to_all | solution.py:128
  287.0 4.8 gather_fusion
  291.9 5.2 reshape.277
  297.0 5.6 multiply_reduce_fusion.2
  302.7 6.9 scatter_custom_fusion.2
  309.6 7.5 scatter_custom_fusion.3
  317.2 55.0 %all_to_all.20 = bf16[4,376,768]{2,1,0:T(8,128)(2,1)S(1)} all-to-all(bf16[4,376,768]{2,1,0:T(8,128)(2,1)S(1)} %bitcast.122), channel_id=1, replica_groups=mesh['expert'=4,'shard'=8] {'expert'}, dimensions={0} | all-to-all | bytes 4620288 | tf_op jit(solution)/shard_map/all_to_all | solution.py:143
  372.1 23.0 %add_convert_fusion = bf16[1504,3072]{1,0:T(8,128)(2,1)} fusion(f32[1504,3072]{1,0:T(8,128)} %get-tuple-element.31, f32[1504,3072]{1,0:T(8,128)} %get-tuple-element.43, bf16[1504,768]{1,0:T(8,128)(2,1)S(1)} %bitcast.125, bf16[1,3072,768]{2,1,0:T(8,128)(2,1)} %all-gather.12.cloned.1.call-done), kind=kOutput, calls=%fused_computation.8 | convolution fusion | flops 7161446400 | bytes 53231616 | tf_op jit(solution)/shard_map/dot_general | solution.py:163
  395.1 12.4 %fusion.16 = bf16[1504,768]{1,0:T(8,128)(2,1)} fusion(bf16[1504,3072]{1,0:T(8,128)(2,1)} %add_convert_fusion, bf16[1,768,3072]{2,1,0:T(8,128)(2,1)} %all-gather.10.cloned.1.call-done), kind=kOutput, calls=%fused_computation.46 | convolution fusion | flops 7097917440 | bytes 16269312 | tf_op jit(solution)/shard_map/dot_general | solution.py:171
  407.5 3.6 all-to-all-start.3
  412.4 50.7 %all-to-all-done.3 = bf16[4,376,768]{2,1,0:T(8,128)(2,1)S(1)} async-done(((bf16[4,376,768]{2,1,0:T(8,128)(2,1)}), bf16[4,376,768]{2,1,0:T(8,128)(2,1)S(1)}, u32[]{:S(2)}, u32[]{:S(2)}) %all-to-all-start.3) | async-done | bytes 2310176 | tf_op jit(solution)/shard_map/all_to_all | solution.py:174
  463.2 4.8 gather_fusion.1
  468.0 5.0 reshape.278
  473.1 7.7 %reduce_sum.190 = f32[591,768]{1,0:T(8,128)} reduce(f32[591,2,768]{2,1,0:T(2,128)} %reshape.278, f32[]{:T(128)} %constant.48.clone.1), dimensions={1}, to_apply=%region_17.18 | reduce | flops 453888 | bytes 5446660 | tf_op jit(solution)/shard_map/reduce_sum | solution.py:182
  480.8 2.6 multiply_reduce_fusion.4
  483.4 1.8 fusion.72
  487.4 2.9 reshape.296
  490.3 4.7 copy.129
  495.1 6.1 multiply_reduce_fusion
  501.2 3.6 multiply_convert_fusion.1
  504.8 2.3 convolution_convert_fusion.6
  507.3 3.0 fusion.32
  512.0 4.8 fusion.35
  517.8 5.6 copy.134
  523.4 10.1 %convert_element_type.183 = bf16[591,2304]{0,1:T(8,128)(2,1)} reshape(bf16[3,197,3,12,64]{1,0,4,3,2:T(4,128)(2,1)} %copy.134) | data formatting | bytes 5446656 | tf_op jit(solution)/shard_map/convert_element_type | solution.py:232
  533.5 6.8 convolution_convert_fusion.1
  540.4 1.6 copy-done.21
  542.0 13.3 %fusion.15 = bf16[1,3072,768]{2,1,0:T(8,128)(2,1)} fusion(bf16[1504,3072]{1,0:T(8,128)(2,1)} %get-tuple-element.30, bf16[1504,768]{1,0:T(8,128)(2,1)S(1)} %bitcast.126), kind=kOutput, calls=%fused_computation.41 | convolution fusion | flops 7099121664 | bytes 16269312 | tf_op jit(solution)/shard_map/dot_general | solution.py:160
  555.4 1.8 copy-done.19
  557.2 13.2 %fusion.14 = bf16[1,768,3072]{2,1,0:T(8,128)(2,1)} fusion(bf16[1504,768]{1,0:T(8,128)(2,1)S(1)} %bitcast.124, bf16[1504,3072]{1,0:T(8,128)(2,1)} %add_convert_fusion), kind=kOutput, calls=%fused_computation.40 | convolution fusion | flops 7099121664 | bytes 16269312 | tf_op jit(solution)/shard_map/dot_general | solution.py:168
  572.1 5.7 fusion.31
  578.8 12.6 %all-reduce.5 = (bf16[768]{0:T(1024)(128)(2,1)S(1)}, bf16[768]{0:T(1024)(128)(2,1)S(1)}) all-reduce(bf16[768]{0:T(1024)(128)(2,1)S(1)} %get-tuple-element.13, bf16[768]{0:T(1024)(128)(2,1)S(1)} %get-tuple-element.9), channel_id=5, replica_groups=mesh['expert'=4,'shard'=8] {'shard'}, use_global_device_ids=true, to_apply=%region_33.34.clone | all-reduce | flops 1536 | bytes 6144
  591.5 9.4 %all-reduce.7 = (bf16[96,4]{0,1:T(4,128)(2,1)S(1)}, bf16[96]{0:T(256)(128)(2,1)S(1)}, bf16[96]{0:T(256)(128)(2,1)S(1)}) all-reduce(bf16[96,4]{0,1:T(4,128)(2,1)S(1)} %copy.140, bf16[96]{0:T(256)(128)(2,1)S(1)} %dynamic-slice.3, bf16[96]{0:T(256)(128)(2,1)S(1)} %dynamic-slice.5), channel_id=1, replica_groups=mesh['expert'=4,'shard'=8] {'expert'}, use_global_device_ids=true, to_apply=%region_31.32 | all-reduce | flops 576 | bytes 2304 | tf_op jit(solution)/shard_map/psum | solution.py:271
  602.5 3.1 add_convert_fusion.1
  605.6 45.3 %reduce-scatter.14.cloned.1.call-done = bf16[1,384,768]{2,1,0:T(8,128)(2,1)} async-done(((bf16[1,3072,768]{2,1,0:T(8,128)(2,1)}), bf16[1,384,768]{2,1,0:T(8,128)(2,1)}) %reduce-scatter.14.cloned.1.call-update) | async-done | bytes 589840 | tf_op jit(solution)/shard_map/reduce_scatter | solution.py:247
  650.9 2.2 convert_element_type.200
  653.1 55.1 %reduce-scatter.12.cloned.1.call-done = bf16[1,96,3072]{2,1,0:T(8,128)(2,1)} async-done(((bf16[1,768,3072]{2,1,0:T(8,128)(2,1)}), bf16[1,96,3072]{2,1,0:T(8,128)(2,1)}) %reduce-scatter.12.cloned.1.call-update) | async-done | bytes 589840 | tf_op jit(solution)/shard_map/reduce_scatter | solution.py:244
  708.2 2.2 convert_element_type.197
  710.4 39.9 %all-reduce.11.cloned.1.call-done = (bf16[96,2304]{1,0:T(8,128)(2,1)}, bf16[96,768]{1,0:T(8,128)(2,1)}) async-done(((bf16[96,2304]{1,0:T(8,128)(2,1)}, bf16[96,768]{1,0:T(8,128)(2,1)}), (bf16[96,2304]{1,0:T(8,128)(2,1)}, bf16[96,768]{1,0:T(8,128)(2,1)})) %all-reduce.11.cloned.1.call-update) | async-done | bytes 589840 | tf_op jit(solution)/shard_map/psum | solution.py:269
  750.2 2.0 convert_element_type.186
  752.2 1.6 convert_element_type.188
  (188 shorter events, 26.2 us)
Async XLA Ops:
  7.2 25.7 %copy-start.31 = (s32[591,2]{0,1:T(2,128)S(1)}, s32[591,2]{0,1:T(2,128)}, u32[]{:S(2)}) copy-start(s32[591,2]{0,1:T(2,128)} %param.13) | copy-start | bytes 14188
  7.2 26.3 %copy-start.5 = (bf16[591,768]{1,0:T(8,128)(2,1)S(1)}, bf16[591,768]{1,0:T(8,128)(2,1)}, u32[]{:S(2)}) copy-start(bf16[591,768]{1,0:T(8,128)(2,1)} %param.11) | copy-start | bytes 2723332
  7.2 39.4 %all-gather.6.cloned.1.call-start = ((), (), s32[]{:S(2)}) async-start(), calls=%async_computation.9 | async-start | bytes 3981312 | tf_op jit(solution)/shard_map/all_gather | solution.py:54
  7.9 84.1 %all-gather.8.cloned.1.call-start = ((), (), s32[]{:S(2)}) async-start(), calls=%async_computation.10 | async-start | bytes 1327104 | tf_op jit(solution)/shard_map/all_gather | solution.py:55
  8.7 109.5 %all-gather.10.cloned.1.call-start = ((), (), s32[]{:S(2)}) async-start(), calls=%async_computation.11 | async-start | bytes 5308416 | tf_op jit(solution)/shard_map/all_gather | solution.py:63
  28.6 23.9 %copy-start.39 = (f32[768]{0:T(1024)}, f32[768]{0:T(1024)S(1)}, u32[]{:S(2)}) copy-start(f32[768]{0:T(1024)S(1)} %convert_element_type.161) | copy-start | bytes 9220
  28.6 74.4 %copy-start.27 = (f32[768]{0:T(1024)}, f32[768]{0:T(1024)S(1)}, u32[]{:S(2)}) copy-start(f32[768]{0:T(1024)S(1)} %convert_element_type.168) | copy-start | bytes 9220
  33.5 61.5 %copy-start.44 = (s32[591]{0:T(1024)}, s32[591]{0:T(1024)S(1)}, u32[]{:S(2)}) copy-start(s32[591]{0:T(1024)S(1)} %get-tuple-element.16) | copy-start | bytes 7096
  33.5 69.5 %copy-start.43 = (s32[591]{0:T(1024)}, s32[591]{0:T(1024)S(1)}, u32[]{:S(2)}) copy-start(s32[591]{0:T(1024)S(1)} %get-tuple-element.15) | copy-start | bytes 7096
  33.8 18.8 %copy-start.33 = (f32[591]{0:T(1024)}, f32[591]{0:T(1024)S(1)}, u32[]{:S(2)}) copy-start(f32[591]{0:T(1024)S(1)} %broadcast_multiply_fusion.3) | copy-start | bytes 7096
  34.2 18.4 %copy-start.35 = (f32[591]{0:T(1024)}, f32[591]{0:T(1024)S(1)}, u32[]{:S(2)}) copy-start(f32[591]{0:T(1024)S(1)} %fusion.30) | copy-start | bytes 7096
  34.2 18.4 %copy-start.41 = (f32[591]{0:T(1024)}, f32[591]{0:T(1024)S(1)}, u32[]{:S(2)}) copy-start(f32[591]{0:T(1024)S(1)} %fusion.62) | copy-start | bytes 7096
  80.4 5.1 copy-start.7
  83.9 2.9 copy-start
  86.8 0.6 copy-start.22
  94.6 8.4 %copy-start.1 = (f32[591,768]{1,0:T(8,128)}, f32[591,768]{1,0:T(8,128)S(1)}, u32[]{:S(2)}) copy-start(f32[591,768]{1,0:T(8,128)S(1)} %get-tuple-element.42) | copy-start | bytes 5446660
  94.7 8.4 %copy-start.25 = (f32[591]{0:T(1024)}, f32[591]{0:T(1024)S(1)}, u32[]{:S(2)}) copy-start(f32[591]{0:T(1024)S(1)} %broadcast_multiply_fusion.2) | copy-start | bytes 7096
  95.0 18.0 %copy-start.37 = (f32[591]{0:T(1024)}, f32[591]{0:T(1024)S(1)}, u32[]{:S(2)}) copy-start(f32[591]{0:T(1024)S(1)} %multiply_reduce_fusion.6) | copy-start | bytes 7096
  95.0 18.0 %copy-start.29 = (f32[591]{0:T(1024)}, f32[591]{0:T(1024)S(1)}, u32[]{:S(2)}) copy-start(f32[591]{0:T(1024)S(1)} %fusion.63) | copy-start | bytes 7096
  113.0 57.8 %all-to-all-start = ((bf16[4,376,768]{2,1,0:T(8,128)(2,1)}), bf16[4,376,768]{2,1,0:T(8,128)(2,1)S(1)}, u32[]{:S(2)}, u32[]{:S(2)}) async-start(bf16[4,376,768]{2,1,0:T(8,128)(2,1)} %bitcast.121), calls=%async_computation | async-start | bytes 4620288 | tf_op jit(solution)/shard_map/all_to_all | solution.py:113
  117.6 101.1 %all-gather.12.cloned.1.call-start = ((), (), s32[]{:S(2)}) async-start(), calls=%async_computation.12 | async-start | bytes 5308416 | tf_op jit(solution)/shard_map/all_gather | solution.py:64
  170.8 47.9 %copy-start.18 = (bf16[4,376,768]{2,1,0:T(8,128)(2,1)}, bf16[4,376,768]{2,1,0:T(8,128)(2,1)S(1)}, u32[]{:S(2)}) copy-start(bf16[4,376,768]{2,1,0:T(8,128)(2,1)S(1)} %all-to-all-done) | copy-start | bytes 6930436
  231.0 3.8 copy-start.45
  231.0 15.8 %copy-start.15 = (bf16[591,768]{1,0:T(8,128)(2,1)S(1)}, bf16[591,768]{1,0:T(8,128)(2,1)}, u32[]{:S(2)}) copy-start(bf16[591,768]{1,0:T(8,128)(2,1)} %param.21) | copy-start | bytes 2723332
  231.0 56.1 %all-to-all-start.1 = ((bf16[4,376,768]{2,1,0:T(8,128)(2,1)}), bf16[4,376,768]{2,1,0:T(8,128)(2,1)S(1)}, u32[]{:S(2)}, u32[]{:S(2)}) async-start(bf16[4,376,768]{2,1,0:T(8,128)(2,1)} %bitcast.128), calls=%async_computation.1 | async-start | bytes 4620288 | tf_op jit(solution)/shard_map/all_to_all | solution.py:128
  234.7 13.6 %copy-start.26 = (f32[591]{0:T(1024)S(1)}, f32[591]{0:T(1024)}, u32[]{:S(2)}) copy-start(f32[591]{0:T(1024)} %copy-done.25) | copy-start | bytes 7096
  234.8 13.6 %copy-start.28 = (f32[768]{0:T(1024)S(1)}, f32[768]{0:T(1024)}, u32[]{:S(2)}) copy-start(f32[768]{0:T(1024)} %copy-done.27) | copy-start | bytes 9220
  234.8 13.5 %copy-start.30 = (f32[591]{0:T(1024)S(1)}, f32[591]{0:T(1024)}, u32[]{:S(2)}) copy-start(f32[591]{0:T(1024)} %copy-done.29) | copy-start | bytes 7096
  245.9 2.4 copy-start.2
  248.3 0.7 copy-start.32
  291.9 5.2 copy-start.13
  372.1 23.0 %copy-start.20 = (bf16[4,376,768]{2,1,0:T(8,128)(2,1)}, bf16[4,376,768]{2,1,0:T(8,128)(2,1)S(1)}, u32[]{:S(2)}) copy-start(bf16[4,376,768]{2,1,0:T(8,128)(2,1)S(1)} %all_to_all.20) | copy-start | bytes 6930436
  407.5 55.7 %all-to-all-start.3 = ((bf16[4,376,768]{2,1,0:T(8,128)(2,1)}), bf16[4,376,768]{2,1,0:T(8,128)(2,1)S(1)}, u32[]{:S(2)}, u32[]{:S(2)}) async-start(bf16[4,376,768]{2,1,0:T(8,128)(2,1)} %bitcast.127), calls=%async_computation.3 | async-start | bytes 4620288 | tf_op jit(solution)/shard_map/all_to_all | solution.py:174
  411.1 160.2 %reduce-scatter.16.cloned.1.call-start = ((), (), s32[]{:S(2)}) async-start(), calls=%async_computation.17 | async-start | bytes 221184
  412.4 190.1 %reduce-scatter.10.cloned.1.call-start = ((), (), s32[]{:S(2)}) async-start(), calls=%async_computation.14 | async-start | bytes 1327104 | tf_op jit(solution)/shard_map/reduce_scatter | solution.py:255
  473.1 7.7 %copy-start.3 = (f32[591,768]{1,0:T(8,128)S(1)}, f32[591,768]{1,0:T(8,128)}, u32[]{:S(2)}) copy-start(f32[591,768]{1,0:T(8,128)} %copy-done.1) | copy-start | bytes 5446660
  480.8 2.6 copy-start.38
  480.8 2.6 copy-start.14
  483.4 3.0 copy-start.16
  483.4 3.0 copy-start.46
  485.2 1.2 copy-start.11
  490.3 4.7 copy-start.23
  490.3 10.9 %slice-start = ((s8[7372800]{0:T(1024)(128)(4,1)}), s8[3178496]{0:T(1024)(128)(4,1)S(1)}, s32[]{:S(2)}) async-start(s8[7372800]{0:T(1024)(128)(4,1)} %bitcast.117), calls=%async_computation.19 | async-start | bytes 6356992
  495.1 6.1 slice-start.1
  501.2 3.6 copy-start.12
  501.2 3.6 copy-start.17
  501.2 3.6 copy-start.24
  504.8 2.4 copy-start.10
  507.2 3.1 copy-start.9
  507.2 95.3 %reduce-scatter.8.cloned.1.call-start = ((), (), s32[]{:S(2)}) async-start(), calls=%async_computation.13 | async-start | bytes 3981312 | tf_op jit(solution)/shard_map/reduce_scatter | solution.py:252
  507.2 3.5 copy-start.4
  510.7 1.3 copy-start.8
  523.4 10.1 %copy-start.6 = (bf16[591,768]{1,0:T(8,128)(2,1)S(1)}, bf16[591,768]{1,0:T(8,128)(2,1)}, u32[]{:S(2)}) copy-start(bf16[591,768]{1,0:T(8,128)(2,1)} %param.11) | copy-start | bytes 2723332
  523.4 10.1 %copy-start.34 = (f32[591]{0:T(1024)S(1)}, f32[591]{0:T(1024)}, u32[]{:S(2)}) copy-start(f32[591]{0:T(1024)} %copy-done.33) | copy-start | bytes 7096
  523.4 10.1 %copy-start.40 = (f32[768]{0:T(1024)S(1)}, f32[768]{0:T(1024)}, u32[]{:S(2)}) copy-start(f32[768]{0:T(1024)} %copy-done.39) | copy-start | bytes 9220
  523.4 10.1 %copy-start.42 = (f32[591]{0:T(1024)S(1)}, f32[591]{0:T(1024)}, u32[]{:S(2)}) copy-start(f32[591]{0:T(1024)} %copy-done.41) | copy-start | bytes 7096
  540.3 1.7 copy-start.21
  540.3 110.6 %reduce-scatter.14.cloned.1.call-start = ((), (), s32[]{:S(2)}) async-start(), calls=%async_computation.16 | async-start | bytes 5308416 | tf_op jit(solution)/shard_map/reduce_scatter | solution.py:247
  555.3 1.8 copy-start.19
  555.4 152.8 %reduce-scatter.12.cloned.1.call-start = ((), (), s32[]{:S(2)}) async-start(), calls=%async_computation.15 | async-start | bytes 5308416 | tf_op jit(solution)/shard_map/reduce_scatter | solution.py:244
  570.4 179.9 %all-reduce.11.cloned.1.call-start = ((), (), s32[]{:S(2)}) async-start(), calls=%async_computation.18 | async-start | bytes 1179648 | tf_op jit(solution)/shard_map/psum | solution.py:269
  572.1 5.7 copy-start.36
Sparse Core Ops, SparseCore 0:
  9.9 36.6 all-gather.5
  48.5 23.9 all-gather.7
  74.3 38.7 all-gather.9
  119.9 39.2 all-gather.11
  415.2 34.1 reduce-scatter.15
  507.3 34.8 reduce-scatter.9
  545.6 48.0 reduce-scatter.7
  597.2 53.7 reduce-scatter.13
  654.4 53.7 reduce-scatter.11
  710.5 39.7 all-reduce.10
where the time goes:
time: 769 us; the launch traced here: 761 us
  waiting for transfers between devices  297 us (39%)
  matrix products  170 us (22%)
  local copies, waits for them, and re-layouts  104 us (14%)
  blocking collectives  102 us (13%)
  other arithmetic  58.9 us (8%)
  between operations  17.1 us (2%)
  starting transfers between devices  12.6 us (2%)
    reduce_scatter x1, waiting for transfers between devices, shards(): lax.psum_scatter(grad_first[None].astype(jnp.bfloat16), 'shard', scatter_...  55.1 us
    all_to_all x1, blocking collectives, shards(): lax.all_to_all(back_out.reshape(experts, capacity, width), 'expert', spli...  55 us
    all_to_all x1, waiting for transfers between devices, shards(): lax.all_to_all(outgoing, 'expert', split_axis=0, concat_axis=0, tiled=True)  52.6 us
    all_to_all x1, waiting for transfers between devices, shards(): lax.all_to_all(row_grad.reshape(experts, capacity, width), 'expert', spli...  50.7 us
    dot_general x1, matrix products, shards(): jnp.dot(flat_rows, expert_first, preferred_element_type=jnp.float32)  47.9 us
    reduce_scatter x1, waiting for transfers between devices, shards(): lax.psum_scatter(grad_second[None].astype(jnp.bfloat16), 'shard', scatter...  45.3 us
    psum x1, waiting for transfers between devices, shards(): lax.psum(shares[0].astype(jnp.bfloat16), 'expert').astype(jnp.float32)  39.9 us
    all_to_all x1, waiting for transfers between devices, shards(): lax.all_to_all(produced, 'expert', split_axis=0, concat_axis=0, tiled=True)  38 us
  transfers between devices with their start and end apart: 13, of which 7 were waited for; matrix products, arithmetic and copies ran while one was open for 32% of the time, Pallas kernels for 0%

commit v1 on v0

--- a/solution.py
+++ b/solution.py
@@ -266,7 +266,9 @@
         ).astype(jnp.float32),
     )
     totals = (
-        lax.psum(shares[0].astype(jnp.bfloat16), "expert").astype(jnp.float32),
+        jnp.sum(lax.all_gather(shares[0].astype(jnp.bfloat16), "expert"), axis=0).astype(
+            jnp.float32
+        ),
         lax.psum(shares[1].astype(jnp.bfloat16), "expert").astype(jnp.float32),
         lax.psum(shares[2].astype(jnp.bfloat16), "expert").astype(jnp.float32),
         lax.psum(shares[3].astype(jnp.bfloat16), "expert").astype(jnp.float32),

time: 769 us -> 841 us (1.094)
  waiting for transfers between devices: 297 us -> 367 us
    all_gather x0 -> x1, waiting for transfers between devices: none -> 39.7 us  [shards(): lax.all_gather(shares[0].astype(jnp.bfloat16), 'expert')]
    psum x1, waiting for transfers between devices: 39.9 us -> 0.42 us  [shards(): lax.psum(shares[1].astype(jnp.bfloat16), 'expert').astype(jnp.float32)]
    unnamed x11 -> x12, waiting for transfers between devices: 2.73 us -> 40 us
    reduce_scatter x1, waiting for transfers between devices: 0.01 us -> 21.9 us  [shards(): lax.psum_scatter(grad_qkv.astype(jnp.bfloat16), 'shard', scatter_dimensio...]
    reduce_scatter x1, waiting for transfers between devices: 45.3 us -> 55.6 us  [shards(): lax.psum_scatter(grad_second[None].astype(jnp.bfloat16), 'shard', scatter...]
    unnamed x113 -> x107, local copies, waits for them, and re-layouts: 24.7 us -> 24.8 us
  transfers between devices with their start and end apart: 13 -> 14, of which waited for: 7 -> 10; matrix products, arithmetic and copies ran while one was open for 32% -> 24% of each run, Pallas kernels for 0% -> 0%
where the time goes in v1:
time: 841 us; the launch traced here: 833 us
  waiting for transfers between devices  367 us (44%)
  matrix products  168 us (20%)
  blocking collectives  104 us (12%)
  local copies, waits for them, and re-layouts  103 us (12%)
  other arithmetic  62.4 us (7%)
  between operations  16.7 us (2%)
  starting transfers between devices  12.4 us (1%)
    reduce_scatter x1, waiting for transfers between devices, shards(): lax.psum_scatter(grad_second[None].astype(jnp.bfloat16), 'shard', scatter...  55.6 us
    all_to_all x1, blocking collectives, shards(): lax.all_to_all(back_out.reshape(experts, capacity, width), 'expert', spli...  55 us
    reduce_scatter x1, waiting for transfers between devices, shards(): lax.psum_scatter(grad_first[None].astype(jnp.bfloat16), 'shard', scatter_...  54.9 us
    all_to_all x1, waiting for transfers between devices, shards(): lax.all_to_all(outgoing, 'expert', split_axis=0, concat_axis=0, tiled=True)  52.6 us
    all_to_all x1, waiting for transfers between devices, shards(): lax.all_to_all(row_grad.reshape(experts, capacity, width), 'expert', spli...  51.9 us
    dot_general x1, matrix products, shards(): jnp.dot(flat_rows, expert_first, preferred_element_type=jnp.float32)  47.9 us
    unnamed x12, waiting for transfers between devices  40 us
    all_gather x1, waiting for transfers between devices, shards(): lax.all_gather(shares[0].astype(jnp.bfloat16), 'expert')  39.7 us
  transfers between devices with their start and end apart: 14, of which 10 were waited for; matrix products, arithmetic and copies ran while one was open for 24% of the time, Pallas kernels for 0%

profile of v1, /device:TPU:0, one launch (start us, length us, event | category | flops | bytes accessed | tf_op | source)
XLA Modules:
  0.0 833.3 jit_solution(9011812009175649418)
XLA Ops:
  13.1 15.5 %all-reduce.6 = (bf16[768]{0:T(1024)(128)(2,1)S(1)}, bf16[768]{0:T(1024)(128)(2,1)S(1)}) all-reduce(bf16[768]{0:T(1024)(128)(2,1)S(1)} %dynamic-update-slice, bf16[768]{0:T(1024)(128)(2,1)S(1)} %dynamic-update-slice.1), channel_id=1, replica_groups=mesh['expert'=4,'shard'=8] {'shard'}, use_global_device_ids=true, to_apply=%add.1 | all-reduce | flops 1536 | bytes 6144
  34.2 12.4 %all-gather.8.cloned.1.call-done = bf16[768,2304]{1,0:T(8,128)(2,1)} async-done(((bf16[96,2304]{1,0:T(8,128)(2,1)}), bf16[768,2304]{1,0:T(8,128)(2,1)}) %all-gather.8.cloned.1.call-update) | async-done | bytes 3538960 | tf_op jit(solution)/shard_map/all_gather | solution.py:54
  46.6 6.0 convolution_convert_fusion.3
  52.6 9.3 %reshape.296 = bf16[3,197,3,12,64]{4,3,2,1,0:T(8,128)(2,1)} reshape(bf16[591,2304]{1,0:T(8,128)(2,1)} %convolution_convert_fusion.3) | data formatting | bytes 5446656 | tf_op jit(solution)/shard_map/reshape | solution.py:71
  61.8 6.7 fusion.74
  68.5 4.2 copy.146
  72.7 4.2 copy.147
  76.9 3.5 copy.145
  80.4 3.4 multiply_reduce_fusion.1
  83.9 1.6 exponential_reduce_fusion
  87.4 1.6 fusion.34
  90.0 2.1 convert_element_type.169
  92.1 2.6 fusion.76
  95.0 8.0 scatter_custom_fusion
  103.1 9.9 %scatter_custom_fusion.1 = bf16[1504,768]{1,0:T(8,128)(2,1)} fusion(bf16[1504,768]{1,0:T(8,128)(2,1)} %scatter_custom_fusion, s32[591]{0:T(1024)S(1)} %get-tuple-element.15, f32[591,768]{1,0:T(8,128)S(1)} %get-tuple-element.40, f32[768]{0:T(1024)S(1)} %convert_element_type.170, f32[591]{0:T(1024)S(1)} %fusion.63, f32[591]{0:T(1024)S(1)} %broadcast_multiply_fusion.2), kind=kCustom, calls=%fused_computation.155 | custom fusion | flops 1815552 | bytes 4141056 | tf_op jit(solution)/shard_map/scatter | solution.py:110
  113.0 4.6 all-to-all-start
  118.2 52.6 %all-to-all-done = bf16[4,376,768]{2,1,0:T(8,128)(2,1)S(1)} async-done(((bf16[4,376,768]{2,1,0:T(8,128)(2,1)}), bf16[4,376,768]{2,1,0:T(8,128)(2,1)S(1)}, u32[]{:S(2)}, u32[]{:S(2)}) %all-to-all-start) | async-done | bytes 2310176 | tf_op jit(solution)/shard_map/all_to_all | solution.py:113
  170.8 47.9 %multiply_convert_fusion = (bf16[1504,3072]{1,0:T(8,128)(2,1)}, f32[1504,3072]{1,0:T(8,128)}, f32[1504,3072]{1,0:T(8,128)}) fusion(bf16[1504,768]{1,0:T(8,128)(2,1)S(1)} %bitcast.124, bf16[1,768,3072]{2,1,0:T(8,128)(2,1)} %all-gather.12.cloned.1.call-done), kind=kOutput, calls=%fused_computation.9 | convolution fusion | flops 7397081088 | bytes 53231616 | tf_op jit(solution)/shard_map/dot_general | solution.py:117
  218.7 12.3 %fusion.19 = bf16[1504,768]{1,0:T(8,128)(2,1)} fusion(bf16[1504,3072]{1,0:T(8,128)(2,1)} %get-tuple-element.28, bf16[1,3072,768]{2,1,0:T(8,128)(2,1)} %all-gather.14.cloned.1.call-done), kind=kOutput, calls=%fused_computation.47 | convolution fusion | flops 7097917440 | bytes 16269312 | tf_op jit(solution)/shard_map/dot_general | solution.py:119
  231.0 3.8 all-to-all-start.1
  234.8 9.4 %all-gather.1 = bf16[8,96,4]{1,2,0:T(4,128)(2,1)S(1)} all-gather(bf16[1,96,4]{1,2,0:T(4,128)(2,1)S(1)} %bitcast.133), channel_id=1, replica_groups=mesh['expert'=4,'shard'=8] {'shard'}, dimensions={0}, use_global_device_ids=true | all-gather | bytes 6912 | tf_op jit(solution)/shard_map/all_gather | solution.py:56
  246.8 1.5 convert_multiply_fusion
  249.6 37.5 %all-to-all-done.1 = bf16[4,376,768]{2,1,0:T(8,128)(2,1)S(1)} async-done(((bf16[4,376,768]{2,1,0:T(8,128)(2,1)}), bf16[4,376,768]{2,1,0:T(8,128)(2,1)S(1)}, u32[]{:S(2)}, u32[]{:S(2)}) %all-to-all-start.1) | async-done | bytes 2310176 | tf_op jit(solution)/shard_map/all_to_all | solution.py:128
  287.0 4.8 gather_fusion
  291.9 5.2 reshape.278
  297.0 5.6 multiply_reduce_fusion.2
  302.7 6.9 scatter_custom_fusion.2
  309.6 7.5 scatter_custom_fusion.3
  317.2 55.0 %all_to_all.20 = bf16[4,376,768]{2,1,0:T(8,128)(2,1)S(1)} all-to-all(bf16[4,376,768]{2,1,0:T(8,128)(2,1)S(1)} %bitcast.123), channel_id=1, replica_groups=mesh['expert'=4,'shard'=8] {'expert'}, dimensions={0} | all-to-all | bytes 4620288 | tf_op jit(solution)/shard_map/all_to_all | solution.py:143
  372.1 23.0 %add_convert_fusion = bf16[1504,3072]{1,0:T(8,128)(2,1)} fusion(f32[1504,3072]{1,0:T(8,128)} %get-tuple-element.29, f32[1504,3072]{1,0:T(8,128)} %get-tuple-element.41, bf16[1504,768]{1,0:T(8,128)(2,1)S(1)} %bitcast.126, bf16[1,3072,768]{2,1,0:T(8,128)(2,1)} %all-gather.14.cloned.1.call-done), kind=kOutput, calls=%fused_computation.8 | convolution fusion | flops 7161446400 | bytes 53231616 | tf_op jit(solution)/shard_map/dot_general | solution.py:163
  395.2 12.4 %fusion.16 = bf16[1504,768]{1,0:T(8,128)(2,1)} fusion(bf16[1504,3072]{1,0:T(8,128)(2,1)} %add_convert_fusion, bf16[1,768,3072]{2,1,0:T(8,128)(2,1)} %all-gather.12.cloned.1.call-done), kind=kOutput, calls=%fused_computation.46 | convolution fusion | flops 7097917440 | bytes 16269312 | tf_op jit(solution)/shard_map/dot_general | solution.py:171
  407.5 3.6 all-to-all-start.3
  411.3 51.9 %all-to-all-done.3 = bf16[4,376,768]{2,1,0:T(8,128)(2,1)S(1)} async-done(((bf16[4,376,768]{2,1,0:T(8,128)(2,1)}), bf16[4,376,768]{2,1,0:T(8,128)(2,1)S(1)}, u32[]{:S(2)}, u32[]{:S(2)}) %all-to-all-start.3) | async-done | bytes 2310176 | tf_op jit(solution)/shard_map/all_to_all | solution.py:174
  463.2 4.8 gather_fusion.1
  468.0 5.0 reshape.279
  473.1 7.7 reduce_sum.204
  480.8 2.6 multiply_reduce_fusion.4
  483.4 1.8 fusion.72
  486.4 2.3 convolution_convert_fusion.6
  488.7 3.4 convolution_convert_fusion.7
  492.2 3.0 reshape.297
  495.2 3.1 copy.129
  498.3 8.8 %multiply_reduce_fusion = (f32[3,12,197]{2,1,0:T(8,128)S(1)}, f32[3,12,197,197]{2,3,1,0:T(8,128)}) fusion(f32[3,12,197,197]{2,3,1,0:T(8,128)} %copy-done, f32[3,12,197]{2,1,0:T(8,128)S(1)} %copy-done.20, bf16[3,197,12,64]{1,3,2,0:T(8,128)(2,1)} %copy.129, bf16[3,197,1,12,64]{1,4,3,0,2:T(8,128)(2,1)} %copy-done.6), kind=kOutput, calls=%fused_computation.24 | convolution fusion | flops 184413264 | bytes 13049280 | tf_op jit(solution)/shard_map/ishd,ithd->ihst/dot_general | solution.py:215
  507.3 6.5 multiply_convert_fusion.1
  516.5 1.4 fusion.35
  518.7 5.6 copy.134
  524.3 9.9 %convert_element_type.185 = bf16[591,2304]{0,1:T(8,128)(2,1)} reshape(bf16[3,197,3,12,64]{1,0,4,3,2:T(4,128)(2,1)} %copy.134) | data formatting | bytes 5446656 | tf_op jit(solution)/shard_map/convert_element_type | solution.py:232
  534.3 6.8 convolution_convert_fusion.1
  544.2 12.5 %fusion.15 = bf16[1,3072,768]{2,1,0:T(8,128)(2,1)} fusion(bf16[1504,3072]{1,0:T(8,128)(2,1)} %get-tuple-element.28, bf16[1504,768]{1,0:T(8,128)(2,1)} %bitcast.127), kind=kOutput, calls=%fused_computation.41 | convolution fusion | flops 7099121664 | bytes 16269312 | tf_op jit(solution)/shard_map/dot_general | solution.py:160
  556.7 1.8 copy-done.17
  558.5 12.9 %fusion.14 = bf16[1,768,3072]{2,1,0:T(8,128)(2,1)} fusion(bf16[1504,768]{1,0:T(8,128)(2,1)S(1)} %bitcast.125, bf16[1504,3072]{1,0:T(8,128)(2,1)} %add_convert_fusion), kind=kOutput, calls=%fused_computation.40 | convolution fusion | flops 7099121664 | bytes 16269312 | tf_op jit(solution)/shard_map/dot_general | solution.py:168
  571.5 21.9 %reduce-scatter.8.cloned.1.call-done = bf16[96,2304]{1,0:T(8,128)(2,1)} async-done(((bf16[768,2304]{1,0:T(8,128)(2,1)}), bf16[96,2304]{1,0:T(8,128)(2,1)}) %reduce-scatter.8.cloned.1.call-update) | async-done | bytes 442384 | tf_op jit(solution)/shard_map/reduce_scatter | solution.py:252
  594.1 36.6 %reduce-scatter.16.cloned.1.call-done = bf16[96,4]{1,0:T(8,128)(2,1)} async-done(((bf16[768,4]{1,0:T(8,128)(2,1)}), bf16[96,4]{1,0:T(8,128)(2,1)}) %reduce-scatter.16.cloned.1.call-update) | async-done | bytes 784
  631.5 5.6 fusion.31
  638.1 12.5 %all-reduce.5 = (bf16[768]{0:T(1024)(128)(2,1)S(1)}, bf16[768]{0:T(1024)(128)(2,1)S(1)}) all-reduce(bf16[768]{0:T(1024)(128)(2,1)S(1)} %get-tuple-element.13, bf16[768]{0:T(1024)(128)(2,1)S(1)} %get-tuple-element.9), channel_id=6, replica_groups=mesh['expert'=4,'shard'=8] {'shard'}, use_global_device_ids=true, to_apply=%region_33.34.clone | all-reduce | flops 1536 | bytes 6144
  650.8 11.7 %all-reduce.7 = (bf16[96,4]{0,1:T(4,128)(2,1)S(1)}, bf16[96]{0:T(256)(128)(2,1)S(1)}, bf16[96]{0:T(256)(128)(2,1)S(1)}) all-reduce(bf16[96,4]{0,1:T(4,128)(2,1)S(1)} %copy.140, bf16[96]{0:T(256)(128)(2,1)S(1)} %dynamic-slice.3, bf16[96]{0:T(256)(128)(2,1)S(1)} %dynamic-slice.5), channel_id=1, replica_groups=mesh['expert'=4,'shard'=8] {'expert'}, use_global_device_ids=true, to_apply=%region_31.32 | all-reduce | flops 576 | bytes 2304 | tf_op jit(solution)/shard_map/psum | solution.py:273
  664.1 3.1 add_convert_fusion.1
  667.6 1.6 convert_element_type.190
  669.2 55.6 %reduce-scatter.14.cloned.1.call-done = bf16[1,384,768]{2,1,0:T(8,128)(2,1)} async-done(((bf16[1,3072,768]{2,1,0:T(8,128)(2,1)}), bf16[1,384,768]{2,1,0:T(8,128)(2,1)}) %reduce-scatter.14.cloned.1.call-update) | async-done | bytes 589840 | tf_op jit(solution)/shard_map/reduce_scatter | solution.py:247
  724.8 2.2 convert_element_type.202
  727.0 54.9 %reduce-scatter.12.cloned.1.call-done = bf16[1,96,3072]{2,1,0:T(8,128)(2,1)} async-done(((bf16[1,768,3072]{2,1,0:T(8,128)(2,1)}), bf16[1,96,3072]{2,1,0:T(8,128)(2,1)}) %reduce-scatter.12.cloned.1.call-update) | async-done | bytes 589840 | tf_op jit(solution)/shard_map/reduce_scatter | solution.py:244
  781.9 2.2 convert_element_type.199
  784.1 39.7 %all-gather.16.cloned.1.call-done = bf16[384,2304]{1,0:T(8,128)(2,1)} async-done(((bf16[96,2304]{1,0:T(8,128)(2,1)}), bf16[384,2304]{1,0:T(8,128)(2,1)}) %all-gather.16.cloned.1.call-update) | async-done | bytes 1769488 | tf_op jit(solution)/shard_map/all_gather | solution.py:269
  823.8 1.8 reduce_sum.250
  (186 shorter events, 30.7 us)
Async XLA Ops:
  7.2 25.7 %copy-start.28 = (s32[591,2]{0,1:T(2,128)S(1)}, s32[591,2]{0,1:T(2,128)}, u32[]{:S(2)}) copy-start(s32[591,2]{0,1:T(2,128)} %param.13) | copy-start | bytes 14188
  7.2 26.3 %copy-start.4 = (bf16[591,768]{1,0:T(8,128)(2,1)S(1)}, bf16[591,768]{1,0:T(8,128)(2,1)}, u32[]{:S(2)}) copy-start(bf16[591,768]{1,0:T(8,128)(2,1)} %param.11) | copy-start | bytes 2723332
  7.2 39.4 %all-gather.8.cloned.1.call-start = ((), (), s32[]{:S(2)}) async-start(), calls=%async_computation.9 | async-start | bytes 3981312 | tf_op jit(solution)/shard_map/all_gather | solution.py:54
  7.9 84.1 %all-gather.10.cloned.1.call-start = ((), (), s32[]{:S(2)}) async-start(), calls=%async_computation.10 | async-start | bytes 1327104 | tf_op jit(solution)/shard_map/all_gather | solution.py:55
  8.7 109.5 %all-gather.12.cloned.1.call-start = ((), (), s32[]{:S(2)}) async-start(), calls=%async_computation.11 | async-start | bytes 5308416 | tf_op jit(solution)/shard_map/all_gather | solution.py:63
  28.6 23.9 %copy-start.36 = (f32[768]{0:T(1024)}, f32[768]{0:T(1024)S(1)}, u32[]{:S(2)}) copy-start(f32[768]{0:T(1024)S(1)} %convert_element_type.163) | copy-start | bytes 9220
  28.6 74.4 %copy-start.24 = (f32[768]{0:T(1024)}, f32[768]{0:T(1024)S(1)}, u32[]{:S(2)}) copy-start(f32[768]{0:T(1024)S(1)} %convert_element_type.170) | copy-start | bytes 9220
  33.5 61.5 %copy-start.41 = (s32[591]{0:T(1024)}, s32[591]{0:T(1024)S(1)}, u32[]{:S(2)}) copy-start(s32[591]{0:T(1024)S(1)} %get-tuple-element.16) | copy-start | bytes 7096
  33.5 69.5 %copy-start.40 = (s32[591]{0:T(1024)}, s32[591]{0:T(1024)S(1)}, u32[]{:S(2)}) copy-start(s32[591]{0:T(1024)S(1)} %get-tuple-element.15) | copy-start | bytes 7096
  33.8 18.8 %copy-start.30 = (f32[591]{0:T(1024)}, f32[591]{0:T(1024)S(1)}, u32[]{:S(2)}) copy-start(f32[591]{0:T(1024)S(1)} %broadcast_multiply_fusion.3) | copy-start | bytes 7096
  34.2 18.4 %copy-start.32 = (f32[591]{0:T(1024)}, f32[591]{0:T(1024)S(1)}, u32[]{:S(2)}) copy-start(f32[591]{0:T(1024)S(1)} %fusion.30) | copy-start | bytes 7096
  34.2 18.4 %copy-start.38 = (f32[591]{0:T(1024)}, f32[591]{0:T(1024)S(1)}, u32[]{:S(2)}) copy-start(f32[591]{0:T(1024)S(1)} %fusion.62) | copy-start | bytes 7096
  80.4 5.1 copy-start.6
  83.9 2.9 copy-start
  86.8 0.6 copy-start.19
  94.6 8.4 %copy-start.1 = (f32[591,768]{1,0:T(8,128)}, f32[591,768]{1,0:T(8,128)S(1)}, u32[]{:S(2)}) copy-start(f32[591,768]{1,0:T(8,128)S(1)} %get-tuple-element.40) | copy-start | bytes 5446660
  94.7 8.4 %copy-start.22 = (f32[591]{0:T(1024)}, f32[591]{0:T(1024)S(1)}, u32[]{:S(2)}) copy-start(f32[591]{0:T(1024)S(1)} %broadcast_multiply_fusion.2) | copy-start | bytes 7096
  95.0 18.0 %copy-start.34 = (f32[591]{0:T(1024)}, f32[591]{0:T(1024)S(1)}, u32[]{:S(2)}) copy-start(f32[591]{0:T(1024)S(1)} %multiply_reduce_fusion.6) | copy-start | bytes 7096
  95.0 18.0 %copy-start.26 = (f32[591]{0:T(1024)}, f32[591]{0:T(1024)S(1)}, u32[]{:S(2)}) copy-start(f32[591]{0:T(1024)S(1)} %fusion.63) | copy-start | bytes 7096
  113.0 57.8 %all-to-all-start = ((bf16[4,376,768]{2,1,0:T(8,128)(2,1)}), bf16[4,376,768]{2,1,0:T(8,128)(2,1)S(1)}, u32[]{:S(2)}, u32[]{:S(2)}) async-start(bf16[4,376,768]{2,1,0:T(8,128)(2,1)} %bitcast.122), calls=%async_computation | async-start | bytes 4620288 | tf_op jit(solution)/shard_map/all_to_all | solution.py:113
  117.6 101.1 %all-gather.14.cloned.1.call-start = ((), (), s32[]{:S(2)}) async-start(), calls=%async_computation.12 | async-start | bytes 5308416 | tf_op jit(solution)/shard_map/all_gather | solution.py:64
  170.8 47.9 %copy-start.16 = (bf16[4,376,768]{2,1,0:T(8,128)(2,1)}, bf16[4,376,768]{2,1,0:T(8,128)(2,1)S(1)}, u32[]{:S(2)}) copy-start(bf16[4,376,768]{2,1,0:T(8,128)(2,1)S(1)} %all-to-all-done) | copy-start | bytes 6930436
  231.0 3.8 copy-start.42
  231.0 15.8 %copy-start.15 = (bf16[591,768]{1,0:T(8,128)(2,1)S(1)}, bf16[591,768]{1,0:T(8,128)(2,1)}, u32[]{:S(2)}) copy-start(bf16[591,768]{1,0:T(8,128)(2,1)} %param.21) | copy-start | bytes 2723332
  231.0 56.1 %all-to-all-start.1 = ((bf16[4,376,768]{2,1,0:T(8,128)(2,1)}), bf16[4,376,768]{2,1,0:T(8,128)(2,1)S(1)}, u32[]{:S(2)}, u32[]{:S(2)}) async-start(bf16[4,376,768]{2,1,0:T(8,128)(2,1)} %bitcast.128), calls=%async_computation.1 | async-start | bytes 4620288 | tf_op jit(solution)/shard_map/all_to_all | solution.py:128
  234.7 13.6 %copy-start.23 = (f32[591]{0:T(1024)S(1)}, f32[591]{0:T(1024)}, u32[]{:S(2)}) copy-start(f32[591]{0:T(1024)} %copy-done.22) | copy-start | bytes 7096
  234.7 13.6 %copy-start.25 = (f32[768]{0:T(1024)S(1)}, f32[768]{0:T(1024)}, u32[]{:S(2)}) copy-start(f32[768]{0:T(1024)} %copy-done.24) | copy-start | bytes 9220
  234.8 13.6 %copy-start.27 = (f32[591]{0:T(1024)S(1)}, f32[591]{0:T(1024)}, u32[]{:S(2)}) copy-start(f32[591]{0:T(1024)} %copy-done.26) | copy-start | bytes 7096
  245.9 2.4 copy-start.2
  248.3 0.7 copy-start.29
  248.6 0.9 copy-start.10
  291.9 5.2 copy-start.13
  372.1 23.0 %copy-start.18 = (bf16[4,376,768]{2,1,0:T(8,128)(2,1)}, bf16[4,376,768]{2,1,0:T(8,128)(2,1)S(1)}, u32[]{:S(2)}) copy-start(bf16[4,376,768]{2,1,0:T(8,128)(2,1)S(1)} %all_to_all.20) | copy-start | bytes 6930436
  407.5 55.7 %all-to-all-start.3 = ((bf16[4,376,768]{2,1,0:T(8,128)(2,1)}), bf16[4,376,768]{2,1,0:T(8,128)(2,1)S(1)}, u32[]{:S(2)}, u32[]{:S(2)}) async-start(bf16[4,376,768]{2,1,0:T(8,128)(2,1)} %bitcast.129), calls=%async_computation.3 | async-start | bytes 4620288 | tf_op jit(solution)/shard_map/all_to_all | solution.py:174
  411.2 132.3 %reduce-scatter.10.cloned.1.call-start = ((), (), s32[]{:S(2)}) async-start(), calls=%async_computation.14 | async-start | bytes 1327104 | tf_op jit(solution)/shard_map/reduce_scatter | solution.py:255
  473.1 7.7 copy-start.3
  480.8 2.6 copy-start.35
  480.8 2.6 copy-start.14
  483.4 3.0 copy-start.21
  485.2 1.2 copy-start.12
  486.4 2.3 copy-start.43
  495.2 3.1 copy-start.20
  498.3 18.1 %slice-start = ((s8[7372800]{0:T(1024)(128)(4,1)}), s8[3178496]{0:T(1024)(128)(4,1)S(1)}, s32[]{:S(2)}) async-start(s8[7372800]{0:T(1024)(128)(4,1)} %bitcast.118), calls=%async_computation.20 | async-start | bytes 6356992
  507.2 86.3 %reduce-scatter.8.cloned.1.call-start = ((), (), s32[]{:S(2)}) async-start(), calls=%async_computation.13 | async-start | bytes 3981312 | tf_op jit(solution)/shard_map/reduce_scatter | solution.py:252
  507.2 6.6 copy-start.9
  507.2 9.2 %slice-start.1 = ((s8[7372800]{0:T(1024)(128)(4,1)}), s8[4194304]{0:T(1024)(128)(4,1)S(1)}, s32[]{:S(2)}) async-start(s8[7372800]{0:T(1024)(128)(4,1)} %bitcast.118), calls=%async_computation.21 | async-start | bytes 8388608
  513.8 1.3 copy-start.8
  515.1 1.3 copy-start.7
  524.3 9.9 %copy-start.5 = (bf16[591,768]{1,0:T(8,128)(2,1)S(1)}, bf16[591,768]{1,0:T(8,128)(2,1)}, u32[]{:S(2)}) copy-start(bf16[591,768]{1,0:T(8,128)(2,1)} %param.11) | copy-start | bytes 2723332
  524.3 9.9 %copy-start.31 = (f32[591]{0:T(1024)S(1)}, f32[591]{0:T(1024)}, u32[]{:S(2)}) copy-start(f32[591]{0:T(1024)} %copy-done.30) | copy-start | bytes 7096
  524.3 9.9 %copy-start.37 = (f32[768]{0:T(1024)S(1)}, f32[768]{0:T(1024)}, u32[]{:S(2)}) copy-start(f32[768]{0:T(1024)} %copy-done.36) | copy-start | bytes 9220
  524.3 9.9 %copy-start.39 = (f32[591]{0:T(1024)S(1)}, f32[591]{0:T(1024)}, u32[]{:S(2)}) copy-start(f32[591]{0:T(1024)} %copy-done.38) | copy-start | bytes 7096
  541.1 1.2 copy-start.11
  541.1 89.6 %reduce-scatter.16.cloned.1.call-start = ((), (), s32[]{:S(2)}) async-start(), calls=%async_computation.19 | async-start | bytes 221184
  543.4 124.2 %all-reduce.10.cloned.1.call-start = ((), (), s32[]{:S(2)}) async-start(), calls=%async_computation.15 | async-start | bytes 294912 | tf_op jit(solution)/shard_map/psum | solution.py:272
  544.1 180.7 %reduce-scatter.14.cloned.1.call-start = ((), (), s32[]{:S(2)}) async-start(), calls=%async_computation.17 | async-start | bytes 5308416 | tf_op jit(solution)/shard_map/reduce_scatter | solution.py:247
  556.6 1.9 copy-start.17
  556.7 225.3 %reduce-scatter.12.cloned.1.call-start = ((), (), s32[]{:S(2)}) async-start(), calls=%async_computation.16 | async-start | bytes 5308416 | tf_op jit(solution)/shard_map/reduce_scatter | solution.py:244
  571.5 252.3 %all-gather.16.cloned.1.call-start = ((), (), s32[]{:S(2)}) async-start(), calls=%async_computation.18 | async-start | bytes 2211840 | tf_op jit(solution)/shard_map/all_gather | solution.py:269
  631.5 5.6 copy-start.33
Sparse Core Ops, SparseCore 0:
  9.9 36.6 all-gather.7
  48.5 23.9 all-gather.9
  74.3 38.7 all-gather.11
  119.9 39.2 all-gather.13
  507.3 34.8 reduce-scatter.9
  545.5 47.9 reduce-scatter.7
  597.1 33.6 reduce-scatter.15
  633.0 34.4 all-reduce.9
  671.0 53.7 reduce-scatter.13
  728.1 53.7 reduce-scatter.11
  783.5 40.2 all-gather.15
